TPU v7x, 32 devices: a whole 2x2x4 slice. The times are simulated.
32 devices in a mesh: freq: 4 (over z), blk: 8 (over y, x, core).
Axes of the slice: x: 2, y: 2, z: 4, core: 2. Of those that a mesh axis runs over, the one named last changes fastest.
Arguments:
- spectra: bfloat16 [8, 512, 2, 32, 128], P('blk', 'freq'), may hold values from -6 to 6
- pair_offsets: int32 [8, 5], P('blk'), may hold values from 0 to 4, as said below
- pair_count: int32 [8], P('blk'), may hold values from 1 to 5, as said below
Outputs:
- correlations: bfloat16 [8, 5, 128, 256, 128], P('blk', None, 'freq')
Inputs may be any that keep to these rules, and one draw needn't show every extreme that they name: `pair_offsets`: for every block, slot 0 holds 0 (the block with itself) and slots 1 to 4 hold the offsets 1 to 4, each once, in an order drawn for each block. `pair_count`: slots at or beyond a block's count are unused; block 0 lists every slot.
All inputs are finite; a program needn't handle non-finite values.
Results may differ from a plain program's by a relative error of at most 0.0052.
Values may be sent and summed in bfloat16 or wider, within the bound.
No kernel may reach another device: no remote copies, remote signals or barrier semaphores. Data moves between devices by JAX's collectives and lax.ppermute only.
A program may use at most 192 MiB of HBM per device.

v0:
```python
import math
import jax
import jax.numpy as jnp
from jax import lax
from jax.sharding import PartitionSpec as P

F = 512
LAGS = 256
REACH = 4
SLOTS = 5


def from_behind(shard, axis, by):
    size = lax.axis_size(axis)
    return lax.ppermute(shard, axis, [(i, (i + by) % size) for i in range(size)])


def lag_table():
    shifted = jnp.arange(LAGS, dtype=jnp.int32) - LAGS // 2
    bins = jnp.arange(F, dtype=jnp.int32) + 1
    phase = jnp.mod(shifted[:, None] * bins[None, :], 2 * F).astype(jnp.float32) * (jnp.pi / F)
    return jnp.stack([jnp.cos(phase), -jnp.sin(phase)], axis=-1).astype(jnp.bfloat16)


def cross_spectrum(home_spec, partner):
    freq_count, parts_count, windows, stations = home_spec.shape
    row_matrix = home_spec.reshape(freq_count, 2 * windows, stations)
    real_part = partner[:, 0]
    imag_part = partner[:, 1]
    real_rows = jnp.concatenate([real_part, imag_part], axis=1)
    imag_rows = jnp.concatenate([imag_part, -real_part], axis=1)
    column_matrix = jnp.concatenate([real_rows, imag_rows], axis=2)
    summed = jnp.einsum(
        "fks,fkt->fst", row_matrix, column_matrix, preferred_element_type=jnp.float32
    )
    return summed / windows


def local(spectra, pair_offsets, pair_count):
    home_spec = spectra[0]
    fetched = [home_spec]
    for offset_step in range(1, REACH + 1):
        fetched.append(from_behind(home_spec, "blk", -offset_step))
    nearby = jnp.stack(fetched)
    partner_offsets = pair_offsets[0]
    listed = pair_count[0]

    def slot_cross(slot_index):
        partner = lax.dynamic_index_in_dim(nearby, partner_offsets[slot_index], 0, keepdims=False)
        cross_term = cross_spectrum(home_spec, partner)
        return jnp.where(slot_index < listed, cross_term, 0.0).astype(jnp.bfloat16)

    crosses = jnp.stack([slot_cross(slot_index) for slot_index in range(SLOTS)])
    lag_weights = lag_table()
    grouped = lax.all_to_all(crosses, "freq", split_axis=2, concat_axis=1, tiled=True)
    count_slots, freq_total, stations_part, double_width = grouped.shape
    regrouped = grouped.reshape(count_slots, freq_total, stations_part, 2, double_width // 2)
    lagged = jnp.einsum(
        "lfr,nfsrt->nslt", lag_weights, regrouped, preferred_element_type=jnp.float32
    )
    result = (lagged * math.sqrt(2.0 / freq_total)).astype(jnp.bfloat16)
    return result[None]


def solution(mesh):
    placed = (P("blk", "freq", None, None, None), P("blk", None), P("blk"))
    return jax.shard_map(
        local,
        mesh=mesh,
        in_specs=placed,
        out_specs=P("blk", None, "freq", None, None),
        check_vma=False,
    )
```

profile of v0, /device:TPU:6, one launch (start us, length us, event | category | flops | bytes accessed | tf_op | source)
XLA Modules:
  0.0 1326.5 jit_solution(1731177960773644525)
XLA Ops:
  0.0 1.4 collective-permute-start.1
  1.4 1.5 collective-permute-start.3
  2.9 1.5 fusion.53
  14.5 3.3 constant_dynamic-update-slice_fusion
  17.9 28.4 %collective-permute-done = bf16[128,2,32,128]{3,2,1,0:T(8,128)(2,1)} collective-permute-done((bf16[128,2,32,128]{3,2,1,0:T(8,128)(2,1)}, bf16[128,2,32,128]{3,2,1,0:T(8,128)(2,1)}, u32[]{:S(2)}, u32[]{:S(2)}) %collective-permute-start) | collective-permute-done | bytes 2097184 | tf_op jit(solution)/shard_map/ppermute | solution.py:15
  46.3 3.3 bitcast_dynamic-update-slice_fusion.8
  49.6 44.5 %collective-permute-done.1 = bf16[128,2,32,128]{3,2,1,0:T(8,128)(2,1)} collective-permute-done((bf16[128,2,32,128]{3,2,1,0:T(8,128)(2,1)}, bf16[128,2,32,128]{3,2,1,0:T(8,128)(2,1)}, u32[]{:S(2)}, u32[]{:S(2)}) %collective-permute-start.1) | collective-permute-done | bytes 2097184 | tf_op jit(solution)/shard_map/ppermute | solution.py:15
  94.1 3.3 bitcast_dynamic-update-slice_fusion.7
  97.4 39.5 %collective-permute-done.2 = bf16[128,2,32,128]{3,2,1,0:T(8,128)(2,1)} collective-permute-done((bf16[128,2,32,128]{3,2,1,0:T(8,128)(2,1)}, bf16[128,2,32,128]{3,2,1,0:T(8,128)(2,1)}, u32[]{:S(2)}, u32[]{:S(2)}) %collective-permute-start.2) | collective-permute-done | bytes 2097184 | tf_op jit(solution)/shard_map/ppermute | solution.py:15
  137.0 3.3 bitcast_dynamic-update-slice_fusion.6
  140.3 21.1 %collective-permute-done.3 = bf16[128,2,32,128]{3,2,1,0:T(8,128)(2,1)S(1)} collective-permute-done((bf16[128,2,32,128]{3,2,1,0:T(8,128)(2,1)}, bf16[128,2,32,128]{3,2,1,0:T(8,128)(2,1)S(1)}, u32[]{:S(2)}, u32[]{:S(2)}) %collective-permute-start.3) | collective-permute-done | bytes 2097184 | tf_op jit(solution)/shard_map/ppermute | solution.py:15
  161.4 1.7 bitcast_dynamic-update-slice_fusion.5
  163.2 8.0 constant_dynamic-slice_fusion
  171.1 2.4 copy_bitcast_fusion.2
  173.5 1.7 slice_bitcast_fusion.7
  175.7 1.7 slice_bitcast_fusion.9
  177.5 1.7 slice_bitcast_fusion.5
  180.3 1.7 slice_bitcast_fusion.3
  182.1 1.7 slice_bitcast_fusion.1
  183.9 7.0 bitcast_dynamic-update-slice_fusion.4
  191.0 6.8 bitcast_dynamic-update-slice_fusion.3
  197.8 6.9 bitcast_dynamic-update-slice_fusion.2
  204.7 6.9 bitcast_dynamic-update-slice_fusion.1
  211.6 5.4 bitcast_dynamic-update-slice_fusion
  217.0 55.5 %copy.24 = bf16[5,128,128,256]{3,1,0,2:T(8,128)(2,1)} copy(bf16[5,128,128,256]{2,3,1,0:T(8,128)(2,1)} %bitcast_dynamic-update-slice_fusion) | data formatting | bytes 83886080 | tf_op jit(solution)/shard_map/stack | solution.py:53
  272.5 11.4 all-to-all-start
  283.9 2.5 cosine_convert_fusion
  286.4 880.8 %all-to-all-done = bf16[5,128,128,256]{3,1,0,2:T(8,128)(2,1)} async-done(((bf16[5,128,128,256]{3,1,0,2:T(8,128)(2,1)}), bf16[5,128,128,256]{3,1,0,2:T(8,128)(2,1)}, u32[]{:S(2)}, u32[]{:S(2)}) %all-to-all-start) | async-done | bytes 41943072 | tf_op jit(solution)/shard_map/all_to_all | solution.py:55
  1167.2 62.7 %copy.26 = bf16[5,4,128,32,256]{2,1,4,3,0:T(4,128)(2,1)} copy(bf16[5,4,128,32,256]{4,2,0,3,1:T(8,128)(2,1)} %bitcast.43) | data formatting | bytes 83886080 | tf_op jit(solution)/shard_map/all_to_all | solution.py:55
  1229.9 60.3 %reshape.163 = bf16[5,512,32,2,128]{1,4,3,2,0:T(8,128)(2,1)} reshape(bf16[5,4,128,32,256]{2,1,4,3,0:T(4,128)(2,1)} %copy.26) | data formatting | bytes 83886080 | tf_op jit(solution)/shard_map/reshape | solution.py:57
  1290.2 22.1 %fusion.1 = bf16[1,5,32,256,128]{3,4,2,1,0:T(8,128)(2,1)} fusion(bf16[5,512,32,2,128]{1,4,3,2,0:T(8,128)(2,1)} %reshape.163, bf16[256,512,1]{1,0,2:T(8,128)(2,1)S(1)} %get-tuple-element.21, bf16[256,512,1]{1,0,2:T(8,128)(2,1)S(1)} %get-tuple-element.20), kind=kOutput, calls=%fused_computation.7 | convolution fusion | flops 10748166144 | bytes 52953088 | tf_op jit(solution)/shard_map/lfr,nfsrt->nslt/dot_general | solution.py:58
  1312.4 14.2 %copy.27 = bf16[1,5,32,256,128]{4,3,2,1,0:T(8,128)(2,1)} copy(bf16[1,5,32,256,128]{3,4,2,1,0:T(8,128)(2,1)} %fusion.1) | data formatting | bytes 20971520 | tf_op jit(solution)/shard_map/broadcast_in_dim | solution.py:62
  (19 shorter events, 1.9 us)
Async XLA Ops:
  0.0 46.3 %collective-permute-start = (bf16[128,2,32,128]{3,2,1,0:T(8,128)(2,1)}, bf16[128,2,32,128]{3,2,1,0:T(8,128)(2,1)}, u32[]{:S(2)}, u32[]{:S(2)}) collective-permute-start(bf16[128,2,32,128]{3,2,1,0:T(8,128)(2,1)} %bitcast.110), channel_id=1, source_target_pairs={{0,7},{1,0},{2,1},{3,2},{4,3},{5,4},{6,5},{7,6},{8,15},{9,8},{10,9... | collective-permute-start | bytes 6291464 | tf_op jit(solution)/shard_map/ppermute | solution.py:15
  0.0 94.1 %collective-permute-start.1 = (bf16[128,2,32,128]{3,2,1,0:T(8,128)(2,1)}, bf16[128,2,32,128]{3,2,1,0:T(8,128)(2,1)}, u32[]{:S(2)}, u32[]{:S(2)}) collective-permute-start(bf16[128,2,32,128]{3,2,1,0:T(8,128)(2,1)} %bitcast.111), channel_id=1, source_target_pairs={{0,6},{1,7},{2,0},{3,1},{4,2},{5,3},{6,4},{7,5},{8,14},{9,15},{10,... | collective-permute-start | bytes 6291464 | tf_op jit(solution)/shard_map/ppermute | solution.py:15
  1.4 135.6 %collective-permute-start.2 = (bf16[128,2,32,128]{3,2,1,0:T(8,128)(2,1)}, bf16[128,2,32,128]{3,2,1,0:T(8,128)(2,1)}, u32[]{:S(2)}, u32[]{:S(2)}) collective-permute-start(bf16[128,2,32,128]{3,2,1,0:T(8,128)(2,1)} %bitcast.112), channel_id=1, source_target_pairs={{0,5},{1,6},{2,7},{3,0},{4,1},{5,2},{6,3},{7,4},{8,13},{9,14},{10,... | collective-permute-start | bytes 6291464 | tf_op jit(solution)/shard_map/ppermute | solution.py:15
  1.4 160.0 %collective-permute-start.3 = (bf16[128,2,32,128]{3,2,1,0:T(8,128)(2,1)}, bf16[128,2,32,128]{3,2,1,0:T(8,128)(2,1)S(1)}, u32[]{:S(2)}, u32[]{:S(2)}) collective-permute-start(bf16[128,2,32,128]{3,2,1,0:T(8,128)(2,1)} %bitcast.113), channel_id=1, source_target_pairs={{0,4},{1,5},{2,6},{3,7},{4,0},{5,1},{6,2},{7,3},{8,12},{9,13},{10,... | collective-permute-start | bytes 6291464 | tf_op jit(solution)/shard_map/ppermute | solution.py:15
  180.2 3.7 copy-start
  190.9 6.8 copy-start.1
  204.7 6.9 copy-start.2
  204.7 6.9 copy-start.3
  272.5 894.7 %all-to-all-start = ((bf16[5,128,128,256]{3,1,0,2:T(8,128)(2,1)}), bf16[5,128,128,256]{3,1,0,2:T(8,128)(2,1)}, u32[]{:S(2)}, u32[]{:S(2)}) async-start(bf16[5,128,128,256]{3,1,0,2:T(8,128)(2,1)} %copy.24), calls=%async_computation | async-start | bytes 83886080 | tf_op jit(solution)/shard_map/all_to_all | solution.py:55
where the time goes:
time: 1330 us
  waiting for transfers between devices  1010 us (76%)
  local copies, waits for them, and re-layouts  229 us (17%)
  matrix products  55.2 us (4%)
  starting transfers between devices  14.4 us (1%)
    all_to_all x1, waiting for transfers between devices, local(): lax.all_to_all(crosses, 'freq', split_axis=2, concat_axis=1, tiled=True)  881 us
    ppermute x4, waiting for transfers between devices, from_behind(): lax.ppermute(shard, axis, [(i, (i + by) % size) for i in range(size)])  134 us
    all_to_all x1, local copies, waits for them, and re-layouts, local(): lax.all_to_all(crosses, 'freq', split_axis=2, concat_axis=1, tiled=True)  62.7 us
    reshape x1, local copies, waits for them, and re-layouts, local(): grouped.reshape(count_slots, freq_total, stations_part, 2, double_width /...  60.3 us
    another operation x1, local copies, waits for them, and re-layouts, local(): crosses = jnp.stack([slot_cross(slot_index) for slot_index in range(SLOTS)])  55.5 us
    dot_general x5, matrix products, cross_spectrum(): jnp.einsum('fks,fkt->fst', row_matrix, column_matrix, preferred_element_t...  33 us
  transfers between devices with their start and end apart: 5, of which 5 were waited for; matrix products, arithmetic and copies ran while one was open for 1% of the time, Pallas kernels for 0%

commit v1 on v0

--- a/solution.py
+++ b/solution.py
@@ -8,6 +8,18 @@
 LAGS = 256
 REACH = 4
 SLOTS = 5
+
+
+def split_up(array, dim, size):
+    shape = array.shape
+    pieces = array.reshape(*shape[:dim], size, shape[dim] // size, *shape[dim + 1 :])
+    return jnp.moveaxis(pieces, dim, 0)
+
+
+def joined_along(blocks, dim):
+    blocks = jnp.moveaxis(blocks, 0, dim)
+    shape = blocks.shape
+    return blocks.reshape(*shape[:dim], shape[dim] * shape[dim + 1], *shape[dim + 2 :])
 
 
 def from_behind(shard, axis, by):
@@ -52,7 +64,14 @@
 
     crosses = jnp.stack([slot_cross(slot_index) for slot_index in range(SLOTS)])
     lag_weights = lag_table()
-    grouped = lax.all_to_all(crosses, "freq", split_axis=2, concat_axis=1, tiled=True)
+    peers, position = (lax.axis_size("freq"), lax.axis_index("freq"))
+    blocks = split_up(crosses, 2, peers)
+    outs = [blocks[position]]
+    for lap in range(1, peers):
+        sent = blocks[position ^ lap]
+        outs.append(lax.ppermute(sent, "freq", [(i_2, i_2 ^ lap) for i_2 in range(peers)]))
+    blocks = jnp.stack(outs)[position ^ jnp.arange(peers)]
+    grouped = joined_along(blocks, 1)
     count_slots, freq_total, stations_part, double_width = grouped.shape
     regrouped = grouped.reshape(count_slots, freq_total, stations_part, 2, double_width // 2)
     lagged = jnp.einsum(

time: 1330 us -> 1480 us (1.11)
  local copies, waits for them, and re-layouts: 229 us -> 333 us
  other arithmetic: 3.15 us -> 64.2 us
    all_to_all x1 -> x0, waiting for transfers between devices: 881 us -> none  [local(): lax.all_to_all(crosses, 'freq', split_axis=2, concat_axis=1, tiled=True)]
    ppermute x0 -> x3, waiting for transfers between devices: none -> 876 us  [local(): lax.ppermute(sent, 'freq', [(i_2, i_2 ^ lap) for i_2 in range(peers)])]
    gather x0 -> x17, local copies, waits for them, and re-layouts: none -> 85.3 us
    all_to_all x1 -> x0, local copies, waits for them, and re-layouts: 62.7 us -> none  [local(): lax.all_to_all(crosses, 'freq', split_axis=2, concat_axis=1, tiled=True)]
    reshape x1 -> x0, local copies, waits for them, and re-layouts: 60.3 us -> none  [local(): grouped.reshape(count_slots, freq_total, stations_part, 2, double_width /...]
    another operation x0 -> x1, local copies, waits for them, and re-layouts: none -> 60.2 us  [local(): grouped.reshape(count_slots, freq_total, stations_part, 2, double_width /...]
    transpose x0 -> x1, local copies, waits for them, and re-layouts: none -> 52.5 us  [joined_along(): blocks = jnp.moveaxis(blocks, 0, dim)]
    unnamed x12 -> x18, local copies, waits for them, and re-layouts: 13.3 us -> 61.9 us
  transfers between devices with their start and end apart: 5 -> 7, of which waited for: 5 -> 6; matrix products, arithmetic and copies ran while one was open for 1% -> 1% of each run, Pallas kernels for 0% -> 0%
where the time goes in v1:
time: 1480 us
  waiting for transfers between devices  1010 us (68%)
  local copies, waits for them, and re-layouts  333 us (22%)
  other arithmetic  64.2 us (4%)
  matrix products  54.7 us (4%)
    ppermute x3, waiting for transfers between devices, local(): lax.ppermute(sent, 'freq', [(i_2, i_2 ^ lap) for i_2 in range(peers)])  876 us
    ppermute x4, waiting for transfers between devices, from_behind(): lax.ppermute(shard, axis, [(i, (i + by) % size) for i in range(size)])  133 us
    unnamed x18, local copies, waits for them, and re-layouts  61.9 us
    another operation x1, local copies, waits for them, and re-layouts, local(): grouped.reshape(count_slots, freq_total, stations_part, 2, double_width /...  60.2 us
    gather x16, local copies, waits for them, and re-layouts  56.3 us
    transpose x1, local copies, waits for them, and re-layouts, joined_along(): blocks = jnp.moveaxis(blocks, 0, dim)  52.5 us
    dot_general x5, matrix products, cross_spectrum(): jnp.einsum('fks,fkt->fst', row_matrix, column_matrix, preferred_element_t...  32.5 us
  transfers between devices with their start and end apart: 7, of which 6 were waited for; matrix products, arithmetic and copies ran while one was open for 1% of the time, Pallas kernels for 0%

profile of v1, /device:TPU:6, one launch (start us, length us, event | category | flops | bytes accessed | tf_op | source)
XLA Modules:
  0.0 1478.8 jit_solution(6036326186744405290)
XLA Ops:
  18.1 28.2 %collective-permute-done = bf16[128,2,32,128]{3,2,1,0:T(8,128)(2,1)} collective-permute-done((bf16[128,2,32,128]{3,2,1,0:T(8,128)(2,1)}, bf16[128,2,32,128]{3,2,1,0:T(8,128)(2,1)}, u32[]{:S(2)}, u32[]{:S(2)}) %collective-permute-start) | collective-permute-done | bytes 2097184 | tf_op jit(solution)/shard_map/ppermute | solution.py:27
  49.6 44.5 %collective-permute-done.1 = bf16[128,2,32,128]{3,2,1,0:T(8,128)(2,1)} collective-permute-done((bf16[128,2,32,128]{3,2,1,0:T(8,128)(2,1)}, bf16[128,2,32,128]{3,2,1,0:T(8,128)(2,1)}, u32[]{:S(2)}, u32[]{:S(2)}) %collective-permute-start.1) | collective-permute-done | bytes 2097184 | tf_op jit(solution)/shard_map/ppermute | solution.py:27
  97.4 39.5 %collective-permute-done.2 = bf16[128,2,32,128]{3,2,1,0:T(8,128)(2,1)} collective-permute-done((bf16[128,2,32,128]{3,2,1,0:T(8,128)(2,1)}, bf16[128,2,32,128]{3,2,1,0:T(8,128)(2,1)}, u32[]{:S(2)}, u32[]{:S(2)}) %collective-permute-start.2) | collective-permute-done | bytes 2097184 | tf_op jit(solution)/shard_map/ppermute | solution.py:27
  140.3 21.1 %collective-permute-done.3 = bf16[128,2,32,128]{3,2,1,0:T(8,128)(2,1)S(1)} collective-permute-done((bf16[128,2,32,128]{3,2,1,0:T(8,128)(2,1)}, bf16[128,2,32,128]{3,2,1,0:T(8,128)(2,1)S(1)}, u32[]{:S(2)}, u32[]{:S(2)}) %collective-permute-start.3) | collective-permute-done | bytes 2097184 | tf_op jit(solution)/shard_map/ppermute | solution.py:27
  163.2 8.0 constant_dynamic-slice_fusion.2
  186.4 6.8 select_convert_fusion.4
  193.2 8.5 constant_dynamic-update-slice_fusion.5
  201.7 6.5 select_convert_fusion.3
  208.2 8.5 constant_dynamic-update-slice_fusion.4
  223.0 8.5 constant_dynamic-update-slice_fusion.3
  231.5 6.5 select_convert_fusion.1
  238.0 8.5 constant_dynamic-update-slice_fusion.2
  246.5 6.5 select_convert_fusion
  252.9 8.5 constant_dynamic-update-slice_fusion.1
  261.4 28.4 %dynamic-slice_bitcast_fusion.3 = (bf16[1,5,128,32,256]{4,3,2,1,0:T(8,128)(2,1)}, bf16[5,128,32,256]{3,2,1,0:T(8,128)(2,1)}, bf16[5,128,32,256]{3,2,1,0:T(8,128)(2,1)}, bf16[5,128,32,256]{3,2,1,0:T(8,128)(2,1)}) fusion(bf16[5,128,4,32,256]{4,3,2,1,0:T(8,128)(2,1)} %constant_dynamic-update-slice_fusion.1, s32[]{:T(128)S(6)} %select_n.110, s32[]{:T(128)S(6)} %select_n.113, ...), kind=kLoop, calls=%fused_computation.17 | loop fusion | bytes 83886096 | tf_op jit(solution)/shard_map/dynamic_slice | solution.py:69
  297.4 223.0 %collective-permute-done.6 = bf16[5,128,32,256]{3,2,1,0:T(8,128)(2,1)} collective-permute-done((bf16[5,128,32,256]{3,2,1,0:T(8,128)(2,1)}, bf16[5,128,32,256]{3,2,1,0:T(8,128)(2,1)}, u32[]{:S(2)}, u32[]{:S(2)}) %collective-permute-start.6) | collective-permute-done | bytes 10485792 | tf_op jit(solution)/shard_map/ppermute | solution.py:72
  520.3 653.0 %collective-permute-done.5 = bf16[5,128,32,256]{3,2,1,0:T(8,128)(2,1)} collective-permute-done((bf16[5,128,32,256]{3,2,1,0:T(8,128)(2,1)}, bf16[5,128,32,256]{3,2,1,0:T(8,128)(2,1)}, u32[]{:S(2)}, u32[]{:S(2)}) %collective-permute-start.5) | collective-permute-done | bytes 10485792 | tf_op jit(solution)/shard_map/ppermute | solution.py:72
  1173.4 28.1 %pad_maximum_fusion = bf16[4,5,128,32,256]{4,3,2,1,0:T(8,128)(2,1)} fusion(bf16[1,5,128,32,256]{4,3,2,1,0:T(8,128)(2,1)} %bitcast.47, bf16[1,5,128,32,256]{4,3,2,1,0:T(8,128)(2,1)} %bitcast.45, bf16[1,5,128,32,256]{4,3,2,1,0:T(8,128)(2,1)} %bitcast.43, bf16[1,5,128,32,256]{4,3,2,1,0:T(8,128)(2,1)} %get-tuple-element.39), kind=kLoop, calls=%fused_computation.4 | loop fusion | flops 62914560 | bytes 83886080 | tf_op jit(solution)/shard_map/stack | solution.py:73
  1201.5 29.1 %fusion.53 = (bf16[4,5,128,32,128]{4,3,2,1,0:T(8,128)(2,1)}, bf16[4,5,128,32,128]{4,3,2,1,0:T(8,128)(2,1)}) fusion(bf16[4,5,128,32,256]{4,3,2,1,0:T(8,128)(2,1)} %pad_maximum_fusion), kind=kLoop, calls=%fused_computation.110 | loop fusion | bytes 83886080 | tf_op jit(solution)/shard_map/gather | solution.py:73
  1230.5 7.3 broadcast.213.clone
  1237.8 28.2 %while.3 = (s32[]{:T(128)}, bf16[4,5,128,32,128]{4,3,2,1,0:T(8,128)(2,1)}, s32[4,1]{0,1:T(1,128)S(1)}, bf16[4,5,128,32,128]{4,3,2,1,0:T(8,128)(2,1)}, s32[]{:T(128)}) while((s32[]{:T(128)}, bf16[4,5,128,32,128]{4,3,2,1,0:T(8,128)(2,1)}, s32[4,1]{0,1:T(1,128)S(1)}, bf16[4,5,128,32,128]{4,3,2,1,0:T(8,128)(2,1)}, s32[]{:T(128)}) %tuple.47), condition=%wide.while_cond.1, body=%wide.while_body.1.sunk | while | flops 2 | bytes 10486357 | solution.py:73
  1238.4 6.5 dynamic-slice_dynamic-update-slice_fusion.5
  1252.5 6.5 dynamic-slice_dynamic-update-slice_fusion.5
  1266.0 7.3 broadcast.213.clone.1
  1273.3 28.1 %while.2 = (s32[]{:T(128)}, bf16[4,5,128,32,128]{4,3,2,1,0:T(8,128)(2,1)}, s32[4,1]{0,1:T(1,128)S(1)}, bf16[4,5,128,32,128]{4,3,2,1,0:T(8,128)(2,1)}, s32[]{:T(128)}) while((s32[]{:T(128)}, bf16[4,5,128,32,128]{4,3,2,1,0:T(8,128)(2,1)}, s32[4,1]{0,1:T(1,128)S(1)}, bf16[4,5,128,32,128]{4,3,2,1,0:T(8,128)(2,1)}, s32[]{:T(128)}) %tuple.53), condition=%wide.while_cond, body=%wide.while_body.sunk | while | flops 2 | bytes 10486357 | solution.py:73
  1280.9 6.5 dynamic-slice_dynamic-update-slice_fusion.4
  1294.9 6.5 dynamic-slice_dynamic-update-slice_fusion.4
  1301.4 28.3 %maximum_bitcast_fusion = bf16[5,4,128,32,256]{4,3,2,0,1:T(8,128)(2,1)} fusion(bf16[4,5,128,32,128]{4,3,2,1,0:T(8,128)(2,1)} %get-tuple-element.20, bf16[4,5,128,32,128]{4,3,2,1,0:T(8,128)(2,1)} %get-tuple-element.12), kind=kLoop, calls=%fused_computation.5 | loop fusion | flops 83886080 | bytes 83886080 | tf_op jit(solution)/shard_map/transpose | solution.py:20
  1329.7 52.5 %copy.9 = bf16[5,4,128,32,256]{2,1,4,3,0:T(4,128)(2,1)} copy(bf16[5,4,128,32,256]{4,3,2,0,1:T(8,128)(2,1)} %maximum_bitcast_fusion) | data formatting | bytes 83886080 | tf_op jit(solution)/shard_map/transpose | solution.py:20
  1382.2 60.2 %reshape_reshape.3 = bf16[5,512,32,2,128]{1,4,3,2,0:T(8,128)(2,1)} reshape(bf16[5,4,128,32,256]{2,1,4,3,0:T(4,128)(2,1)} %copy.9) | data formatting | bytes 83886080 | tf_op jit(solution)/shard_map/reshape;reshape | solution.py:76
  1442.5 22.1 %fusion.1 = bf16[1,5,32,256,128]{3,4,2,1,0:T(8,128)(2,1)} fusion(bf16[5,512,32,2,128]{1,4,3,2,0:T(8,128)(2,1)} %reshape_reshape.3, bf16[256,512,1]{1,0,2:T(8,128)(2,1)S(1)} %copy-done.3, bf16[256,512,1]{1,0,2:T(8,128)(2,1)S(1)} %copy-done.2), kind=kOutput, calls=%fused_computation.13 | convolution fusion | flops 10748166144 | bytes 52953088 | tf_op jit(solution)/shard_map/lfr,nfsrt->nslt/dot_general | solution.py:77
  1464.6 14.2 copy.10
  (52 shorter events, 79.0 us)
Async XLA Ops:
  0.0 46.3 %collective-permute-start = (bf16[128,2,32,128]{3,2,1,0:T(8,128)(2,1)}, bf16[128,2,32,128]{3,2,1,0:T(8,128)(2,1)}, u32[]{:S(2)}, u32[]{:S(2)}) collective-permute-start(bf16[128,2,32,128]{3,2,1,0:T(8,128)(2,1)} %bitcast.126), channel_id=1, source_target_pairs={{0,7},{1,0},{2,1},{3,2},{4,3},{5,4},{6,5},{7,6},{8,15},{9,8},{10,9... | collective-permute-start | bytes 6291464 | tf_op jit(solution)/shard_map/ppermute | solution.py:27
  0.0 94.1 %collective-permute-start.1 = (bf16[128,2,32,128]{3,2,1,0:T(8,128)(2,1)}, bf16[128,2,32,128]{3,2,1,0:T(8,128)(2,1)}, u32[]{:S(2)}, u32[]{:S(2)}) collective-permute-start(bf16[128,2,32,128]{3,2,1,0:T(8,128)(2,1)} %bitcast.127), channel_id=1, source_target_pairs={{0,6},{1,7},{2,0},{3,1},{4,2},{5,3},{6,4},{7,5},{8,14},{9,15},{10,... | collective-permute-start | bytes 6291464 | tf_op jit(solution)/shard_map/ppermute | solution.py:27
  1.4 135.6 %collective-permute-start.2 = (bf16[128,2,32,128]{3,2,1,0:T(8,128)(2,1)}, bf16[128,2,32,128]{3,2,1,0:T(8,128)(2,1)}, u32[]{:S(2)}, u32[]{:S(2)}) collective-permute-start(bf16[128,2,32,128]{3,2,1,0:T(8,128)(2,1)} %bitcast.128), channel_id=1, source_target_pairs={{0,5},{1,6},{2,7},{3,0},{4,1},{5,2},{6,3},{7,4},{8,13},{9,14},{10,... | collective-permute-start | bytes 6291464 | tf_op jit(solution)/shard_map/ppermute | solution.py:27
  1.4 160.0 %collective-permute-start.3 = (bf16[128,2,32,128]{3,2,1,0:T(8,128)(2,1)}, bf16[128,2,32,128]{3,2,1,0:T(8,128)(2,1)S(1)}, u32[]{:S(2)}, u32[]{:S(2)}) collective-permute-start(bf16[128,2,32,128]{3,2,1,0:T(8,128)(2,1)} %bitcast.129), channel_id=1, source_target_pairs={{0,4},{1,5},{2,6},{3,7},{4,0},{5,1},{6,2},{7,3},{8,12},{9,13},{10,... | collective-permute-start | bytes 6291464 | tf_op jit(solution)/shard_map/ppermute | solution.py:27
  171.1 3.2 copy-start
  181.7 4.7 copy-start.1
  289.8 230.5 %collective-permute-start.6 = (bf16[5,128,32,256]{3,2,1,0:T(8,128)(2,1)}, bf16[5,128,32,256]{3,2,1,0:T(8,128)(2,1)}, u32[]{:S(2)}, u32[]{:S(2)}) collective-permute-start(bf16[5,128,32,256]{3,2,1,0:T(8,128)(2,1)} %get-tuple-element.40), channel_id=1, source_target_pairs={{0,24},{8,16},{16,8},{24,0},{1,25},{9,17},{17,9},{25,1},{2,26},{10... | collective-permute-start | bytes 31457288 | tf_op jit(solution)/shard_map/ppermute | solution.py:72
  293.4 879.9 %collective-permute-start.5 = (bf16[5,128,32,256]{3,2,1,0:T(8,128)(2,1)}, bf16[5,128,32,256]{3,2,1,0:T(8,128)(2,1)}, u32[]{:S(2)}, u32[]{:S(2)}) collective-permute-start(bf16[5,128,32,256]{3,2,1,0:T(8,128)(2,1)} %get-tuple-element.41), channel_id=1, source_target_pairs={{0,16},{8,24},{16,0},{24,8},{1,17},{9,25},{17,1},{25,9},{2,18},{10... | collective-permute-start | bytes 31457288 | tf_op jit(solution)/shard_map/ppermute | solution.py:72
  293.4 879.9 %collective-permute-start.4 = (bf16[5,128,32,256]{3,2,1,0:T(8,128)(2,1)}, bf16[5,128,32,256]{3,2,1,0:T(8,128)(2,1)}, u32[]{:S(2)}, u32[]{:S(2)}) collective-permute-start(bf16[5,128,32,256]{3,2,1,0:T(8,128)(2,1)} %get-tuple-element.42), channel_id=1, source_target_pairs={{0,8},{8,0},{16,24},{24,16},{1,9},{9,1},{17,25},{25,17},{2,10},{10... | collective-permute-start | bytes 31457288 | tf_op jit(solution)/shard_map/ppermute | solution.py:72
  1382.2 60.3 %copy-start.2 = (bf16[256,512,1]{1,0,2:T(8,128)(2,1)S(1)}, bf16[256,512,1]{1,0,2:T(8,128)(2,1)}, u32[]{:S(2)}) copy-start(bf16[256,512,1]{1,0,2:T(8,128)(2,1)} %get-tuple-element.58) | copy-start | bytes 786436
  1382.2 60.3 %copy-start.3 = (bf16[256,512,1]{1,0,2:T(8,128)(2,1)S(1)}, bf16[256,512,1]{1,0,2:T(8,128)(2,1)}, u32[]{:S(2)}) copy-start(bf16[256,512,1]{1,0,2:T(8,128)(2,1)} %get-tuple-element.59) | copy-start | bytes 786436
